TPU v7x, 512 devices: a whole 4x4x16 slice. The times are simulated.
512 devices in a mesh: aux: 16 (over z), pair: 32 (over y, x, core).
Axes of the slice: x: 4, y: 4, z: 16, core: 2. Of those that a mesh axis runs over, the one named last changes fastest.
Arguments:
- b_tensor: bfloat16 [2560, 262144], P('aux', 'pair'), may hold values from -0.0625 to 0.0625
- eps_occ: float32 [256], replicated, may hold values from -1 to -0.3
- eps_vir: float32 [1024], replicated, may hold values from 0.05 to 3
- trial: bfloat16 [32, 262144], P(None, 'pair'), may hold values from -6 to 6
Outputs:
- trial_next: float32 [32, 262144], P(None, 'pair')
- residual: bfloat16 [32, 262144], P(None, 'pair')
- subspace: float32 [32, 32], replicated
All inputs are finite; a program needn't handle non-finite values.
Results may differ from a plain program's by a relative error of at most 0.028.
Values may be sent and summed in bfloat16 or wider, within the bound.
No kernel may reach another device: no remote copies, remote signals or barrier semaphores. Data moves between devices by JAX's collectives and lax.ppermute only.
A program may use at most 64 MiB of HBM per device.

v0:
```python
import jax
import jax.numpy as jnp
from jax import lax
from jax.sharding import PartitionSpec as P

ITERS = 2
HIGHEST_PRECISION = lax.Precision.HIGHEST


def correlation_of(first_rows, second_rows):
    return lax.dot_general(
        first_rows,
        second_rows,
        (((1,), (1,)), ((), ())),
        precision=HIGHEST_PRECISION,
        preferred_element_type=jnp.float32,
    )


def product(first_mat, second_mat):
    return jnp.dot(
        first_mat, second_mat, precision=HIGHEST_PRECISION, preferred_element_type=jnp.float32
    )


def global_sum(matrices):
    return lax.psum(matrices, "pair")


def orthonormal(trial_now, gram_now):
    lower_tri = jnp.linalg.cholesky(gram_now)
    inverse = lax.linalg.triangular_solve(
        lower_tri, jnp.eye(gram_now.shape[0], dtype=jnp.float32), left_side=True, lower=True
    )
    return product(inverse, trial_now)


def coupling_of(b_tensor, basis_now):
    basis_low = basis_now.astype(jnp.bfloat16)
    partial_proj = lax.dot_general(
        b_tensor, basis_low, (((1,), (1,)), ((), ())), preferred_element_type=jnp.float32
    )
    projected_low = lax.psum(partial_proj, "pair").astype(jnp.bfloat16)
    partial_value = lax.dot_general(
        projected_low, b_tensor, (((0,), (0,)), ((), ())), preferred_element_type=jnp.float32
    )
    return lax.psum(partial_value.astype(jnp.bfloat16), "aux").astype(jnp.float32)


def on_device(b_tensor, eps_occ, eps_vir, trial):
    block_cols = b_tensor.shape[1]
    npair_all = eps_occ.shape[0] * eps_vir.shape[0]
    everything = (eps_vir[None, :] - eps_occ[:, None]).reshape(npair_all)
    diagonal = lax.dynamic_slice_in_dim(everything, lax.axis_index("pair") * block_cols, block_cols)
    trial_now = trial.astype(jnp.float32)
    diag_row = diagonal[None, :]
    for iteration in range(ITERS):
        gram_now = global_sum(correlation_of(trial_now, trial_now) / npair_all)
        basis_now = orthonormal(trial_now, gram_now)
        image_now = coupling_of(b_tensor, basis_now) + diag_row * basis_now
        subspace = global_sum(correlation_of(image_now, basis_now) / npair_all)
        residual = image_now - product(subspace, basis_now)
        trial_now = basis_now - residual / diag_row
    return (trial_now, residual.astype(jnp.bfloat16), subspace)


def solution(mesh):
    in_specs = (P("aux", "pair"), P(), P(), P(None, "pair"))
    out_specs = (P(None, "pair"), P(None, "pair"), P())
    return jax.shard_map(
        on_device, mesh=mesh, in_specs=in_specs, out_specs=out_specs, check_vma=False
    )
```

profile of v0, /device:TPU:32, one launch (start us, length us, event | category | flops | bytes accessed | tf_op | source)
XLA Modules:
  0.0 1066.8 jit_solution(1206010079620472459)
XLA Ops:
  7.2 1.6 convolution_multiply_fusion.3
  8.8 128.4 %psum.56 = f32[32,32]{0,1:T(8,128)S(1)} all-reduce(f32[32,32]{0,1:T(8,128)S(1)} %convolution_multiply_fusion.3), channel_id=1, replica_groups=mesh['aux'=16,'pair'=32] {'pair'}, use_global_device_ids=true, to_apply=%region_0.0 | all-reduce | flops 1024 | bytes 8192 | tf_op jit(solution)/shard_map/psum | solution.py:27
  137.3 2.9 cholesky.44
  141.6 2.4 custom-call.6
  144.2 1.6 fusion.23
  145.9 1.0 copy-done.1
  147.8 123.9 %psum.57 = bf16[160,32]{0,1:T(8,128)(2,1)S(1)} all-reduce(f32[160,32]{0,1:T(8,128)S(1)} %convolution_bitcast_fusion.1), channel_id=1, replica_groups=mesh['aux'=16,'pair'=32] {'pair'}, use_global_device_ids=true, to_apply=%region_3.6 | all-reduce | flops 5120 | bytes 30720 | tf_op jit(solution)/shard_map/psum | solution.py:43
  271.7 1.3 convolution_convert_fusion.1
  273.3 1.2 copy.16
  275.2 133.4 %all-reduce.3.cloned.1.call-done = bf16[32,8192]{1,0:T(8,128)(2,1)} async-done(((bf16[32,8192]{1,0:T(8,128)(2,1)}), bf16[32,8192]{1,0:T(8,128)(2,1)}) %all-reduce.3.cloned.1.call-update) | async-done | bytes 524304 | tf_op jit(solution)/shard_map/psum | solution.py:47
  408.6 2.9 convolution_multiply_fusion.2
  411.5 123.8 %psum.59 = f32[32,32]{0,1:T(8,128)S(1)} all-reduce(f32[32,32]{0,1:T(8,128)S(1)} %convolution_multiply_fusion.2), channel_id=1, replica_groups=mesh['aux'=16,'pair'=32] {'pair'}, use_global_device_ids=true, to_apply=%region_5.8 | all-reduce | flops 1024 | bytes 8192 | tf_op jit(solution)/shard_map/psum | solution.py:27
  535.3 2.8 fusion.1
  540.0 123.8 %psum.60 = f32[32,32]{0,1:T(8,128)S(1)} all-reduce(f32[32,32]{0,1:T(8,128)S(1)} %convolution_multiply_fusion.1), channel_id=1, replica_groups=mesh['aux'=16,'pair'=32] {'pair'}, use_global_device_ids=true, to_apply=%region_6.9 | all-reduce | flops 1024 | bytes 8192 | tf_op jit(solution)/shard_map/psum | solution.py:27
  663.9 2.9 cholesky.55
  668.1 2.4 custom-call.7
  670.8 2.2 fusion.24
  673.0 1.0 copy-done.2
  675.0 123.8 %psum.61 = bf16[160,32]{0,1:T(8,128)(2,1)S(1)} all-reduce(f32[160,32]{0,1:T(8,128)S(1)} %convolution_bitcast_fusion), channel_id=1, replica_groups=mesh['aux'=16,'pair'=32] {'pair'}, use_global_device_ids=true, to_apply=%region_7.10 | all-reduce | flops 5120 | bytes 30720 | tf_op jit(solution)/shard_map/psum | solution.py:43
  798.7 1.3 convolution_convert_fusion
  800.1 128.7 %all-reduce.5.cloned.1.call-done = bf16[32,8192]{1,0:T(8,128)(2,1)} async-done(((bf16[32,8192]{1,0:T(8,128)(2,1)}), bf16[32,8192]{1,0:T(8,128)(2,1)}) %all-reduce.5.cloned.1.call-update) | async-done | bytes 524304 | tf_op jit(solution)/shard_map/psum | solution.py:47
  928.9 2.8 convolution_multiply_fusion
  931.7 123.8 %psum.63 = f32[32,32]{0,1:T(8,128)S(1)} all-reduce(f32[32,32]{0,1:T(8,128)S(1)} %convolution_multiply_fusion), channel_id=1, replica_groups=mesh['aux'=16,'pair'=32] {'pair'}, use_global_device_ids=true, to_apply=%region_9.12 | all-reduce | flops 1024 | bytes 8192 | tf_op jit(solution)/shard_map/psum | solution.py:27
  1056.1 3.9 fusion.22
  (36 shorter events, 8.8 us)
Async XLA Ops:
  7.2 139.7 %copy-start = (bf16[160,8192]{1,0:T(8,128)(2,1)S(1)}, bf16[160,8192]{1,0:T(8,128)(2,1)}, u32[]{:S(2)}) copy-start(bf16[160,8192]{1,0:T(8,128)(2,1)} %param.7) | copy-start | bytes 7864324
  7.2 401.5 %all-reduce.3.cloned.1.call-start = ((), (), s32[]{:S(2)}) async-start(), calls=%async_computation | async-start | bytes 1048576 | tf_op jit(solution)/shard_map/psum | solution.py:47
  145.9 1.0 copy-start.1
  147.8 125.4 %copy-start.6 = (f32[1024]{0:T(1024)S(1)}, f32[1024]{0:T(1024)}, u32[]{:S(2)}) copy-start(f32[1024]{0:T(1024)} %param.9) | copy-start | bytes 12292
  147.8 125.3 %copy-start.7 = (f32[256]{0:T(256)S(1)}, f32[256]{0:T(256)}, u32[]{:S(2)}) copy-start(f32[256]{0:T(256)} %param.8) | copy-start | bytes 3076
  273.1 655.8 %all-reduce.5.cloned.1.call-start = ((), (), s32[]{:S(2)}) async-start(), calls=%async_computation.1 | async-start | bytes 1048576 | tf_op jit(solution)/shard_map/psum | solution.py:47
  408.6 126.7 %copy-start.4 = (bf16[32,8192]{1,0:T(8,128)(2,1)S(1)}, bf16[32,8192]{1,0:T(8,128)(2,1)}, u32[]{:S(2)}) copy-start(bf16[32,8192]{1,0:T(8,128)(2,1)} %all-reduce.3.cloned.1.call-done) | copy-start | bytes 1572868
  538.1 1.0 copy-start.3
  673.0 1.0 copy-start.2
  928.9 127.3 %copy-start.5 = (bf16[32,8192]{1,0:T(8,128)(2,1)S(1)}, bf16[32,8192]{1,0:T(8,128)(2,1)}, u32[]{:S(2)}) copy-start(bf16[32,8192]{1,0:T(8,128)(2,1)} %all-reduce.5.cloned.1.call-done) | copy-start | bytes 1572868
Sparse Core Ops, SparseCore 0:
  273.2 135.3 all-reduce.2
  800.2 128.5 all-reduce.4
where the time goes:
time: 1070 us
  blocking collectives  747 us (70%)
  waiting for transfers between devices  262 us (24%)
  matrix products  23.8 us (2%)
  between operations  14.2 us (1%)
  other arithmetic  13.5 us (1%)
    psum x4, blocking collectives, global_sum(): return lax.psum(matrices, 'pair')  500 us
    psum x2, waiting for transfers between devices, coupling_of(): lax.psum(partial_value.astype(jnp.bfloat16), 'aux').astype(jnp.float32)  262 us
    psum x2, blocking collectives, coupling_of(): projected_low = lax.psum(partial_proj, 'pair').astype(jnp.bfloat16)  248 us
  transfers between devices with their start and end apart: 2, of which 2 were waited for; matrix products, arithmetic and copies ran while one was open for 0% of the time, Pallas kernels for 0%

commit v1 on v0

--- a/solution.py
+++ b/solution.py
@@ -2,9 +2,15 @@
 import jax.numpy as jnp
 from jax import lax
 from jax.sharding import PartitionSpec as P
+from jax.lax import all_gather
 
 ITERS = 2
 HIGHEST_PRECISION = lax.Precision.HIGHEST
+
+
+def order_the_sectors(xin):
+    response = all_gather(xin, axis_name="pair")
+    return jnp.sum(response, 0)
 
 
 def correlation_of(first_rows, second_rows):
@@ -24,7 +30,7 @@
 
 
 def global_sum(matrices):
-    return lax.psum(matrices, "pair")
+    return order_the_sectors(matrices)
 
 
 def orthonormal(trial_now, gram_now):

time: 1070 us -> 676 us (0.63)
  the two profiles are of different devices: /device:TPU:32 before, /device:TPU:1 now
where the time goes in v1:
time: 676 us; the launch traced here: 675 us
  blocking collectives  367 us (54%)
  waiting for transfers between devices  251 us (37%)
  matrix products  22.9 us (3%)
  other arithmetic  14.8 us (2%)
  between operations  14.2 us (2%)
    psum x2, waiting for transfers between devices, coupling_of(): lax.psum(partial_value.astype(jnp.bfloat16), 'aux').astype(jnp.float32)  251 us
    psum x2, blocking collectives, coupling_of(): projected_low = lax.psum(partial_proj, 'pair').astype(jnp.bfloat16)  242 us
    all_gather x4, blocking collectives, order_the_sectors(): response = all_gather(xin, axis_name='pair')  125 us
  transfers between devices with their start and end apart: 2, of which 2 were waited for; matrix products, arithmetic and copies ran while one was open for 0% of the time, Pallas kernels for 0%

profile of v1, /device:TPU:1, one launch (start us, length us, event | category | flops | bytes accessed | tf_op | source)
XLA Modules:
  0.0 675.4 jit_solution(4837127541710372627)
XLA Ops:
  7.2 1.6 convolution_multiply_fusion.3
  8.9 31.3 %all-gather = f32[1024,32]{1,0:T(8,128)} all-gather(f32[32,32]{1,0:T(8,128)S(1)} %convolution_multiply_fusion.3), channel_id=2, replica_groups=mesh['aux'=16,'pair'=32] {'pair'}, dimensions={0}, use_global_device_ids=true | all-gather | bytes 135168 | tf_op jit(solution)/shard_map/all_gather | solution.py:12
  40.2 1.1 reduce_sum.36
  41.3 2.9 cholesky.44
  45.6 2.4 custom-call.6
  50.8 121.0 %psum.28 = bf16[160,32]{0,1:T(8,128)(2,1)S(1)} all-reduce(f32[160,32]{0,1:T(8,128)S(1)} %convolution_bitcast_fusion.1), channel_id=1, replica_groups=mesh['aux'=16,'pair'=32] {'pair'}, use_global_device_ids=true, to_apply=%region_3.6 | all-reduce | flops 5120 | bytes 30720 | tf_op jit(solution)/shard_map/psum | solution.py:49
  171.8 1.3 convolution_convert_fusion.1
  173.4 1.2 copy.11
  175.3 127.0 %all-reduce.3.cloned.1.call-done = bf16[32,8192]{1,0:T(8,128)(2,1)} async-done(((bf16[32,8192]{1,0:T(8,128)(2,1)}), bf16[32,8192]{1,0:T(8,128)(2,1)}) %all-reduce.3.cloned.1.call-update) | async-done | bytes 524304 | tf_op jit(solution)/shard_map/psum | solution.py:53
  302.4 2.9 convolution_multiply_fusion.2
  305.2 34.8 %all-gather.1 = f32[1024,32]{1,0:T(8,128)S(1)} all-gather(f32[32,32]{1,0:T(8,128)S(1)} %convolution_multiply_fusion.2), channel_id=3, replica_groups=mesh['aux'=16,'pair'=32] {'pair'}, dimensions={0}, use_global_device_ids=true | all-gather | bytes 135168 | tf_op jit(solution)/shard_map/all_gather | solution.py:12
  340.0 2.9 fusion.1
  343.0 1.0 copy-done.3
  344.9 24.3 %all-gather.2 = f32[1024,32]{1,0:T(8,128)S(1)} all-gather(f32[32,32]{1,0:T(8,128)S(1)} %convolution_multiply_fusion.1), channel_id=4, replica_groups=mesh['aux'=16,'pair'=32] {'pair'}, dimensions={0}, use_global_device_ids=true | all-gather | bytes 135168 | tf_op jit(solution)/shard_map/all_gather | solution.py:12
  369.3 2.9 cholesky.55
  373.6 2.4 custom-call.7
  376.3 2.2 fusion.24
  378.5 1.0 copy-done.2
  380.4 120.9 %psum.30 = bf16[160,32]{0,1:T(8,128)(2,1)S(1)} all-reduce(f32[160,32]{0,1:T(8,128)S(1)} %convolution_bitcast_fusion), channel_id=1, replica_groups=mesh['aux'=16,'pair'=32] {'pair'}, use_global_device_ids=true, to_apply=%region_7.10 | all-reduce | flops 5120 | bytes 30720 | tf_op jit(solution)/shard_map/psum | solution.py:49
  501.3 1.3 convolution_convert_fusion
  502.7 124.3 %all-reduce.5.cloned.1.call-done = bf16[32,8192]{1,0:T(8,128)(2,1)} async-done(((bf16[32,8192]{1,0:T(8,128)(2,1)}), bf16[32,8192]{1,0:T(8,128)(2,1)}) %all-reduce.5.cloned.1.call-update) | async-done | bytes 524304 | tf_op jit(solution)/shard_map/psum | solution.py:53
  627.0 2.8 convolution_multiply_fusion
  629.8 34.8 %all-gather.3 = f32[1024,32]{1,0:T(8,128)S(1)} all-gather(f32[32,32]{1,0:T(8,128)S(1)} %convolution_multiply_fusion), channel_id=5, replica_groups=mesh['aux'=16,'pair'=32] {'pair'}, dimensions={0}, use_global_device_ids=true | all-gather | bytes 135168 | tf_op jit(solution)/shard_map/all_gather | solution.py:12
  664.6 4.0 fusion.22
  (39 shorter events, 8.9 us)
Async XLA Ops:
  7.2 42.7 %copy-start = (bf16[160,8192]{1,0:T(8,128)(2,1)S(1)}, bf16[160,8192]{1,0:T(8,128)(2,1)}, u32[]{:S(2)}) copy-start(bf16[160,8192]{1,0:T(8,128)(2,1)} %param.7) | copy-start | bytes 7864324
  7.2 41.1 %copy-start.4 = (bf16[32,8192]{1,0:T(8,128)(2,1)S(1)}, bf16[32,8192]{1,0:T(8,128)(2,1)}, u32[]{:S(2)}) copy-start(bf16[32,8192]{1,0:T(8,128)(2,1)} %param.10) | copy-start | bytes 1572868
  7.2 295.2 %all-reduce.3.cloned.1.call-start = ((), (), s32[]{:S(2)}) async-start(), calls=%async_computation | async-start | bytes 1048576 | tf_op jit(solution)/shard_map/psum | solution.py:53
  48.9 1.0 copy-start.1
  50.8 122.4 %copy-start.6 = (f32[1024]{0:T(1024)S(1)}, f32[1024]{0:T(1024)}, u32[]{:S(2)}) copy-start(f32[1024]{0:T(1024)} %param.9) | copy-start | bytes 12292
  50.8 122.4 %copy-start.7 = (f32[256]{0:T(256)S(1)}, f32[256]{0:T(256)}, u32[]{:S(2)}) copy-start(f32[256]{0:T(256)} %param.8) | copy-start | bytes 3076
  173.2 453.8 %all-reduce.5.cloned.1.call-start = ((), (), s32[]{:S(2)}) async-start(), calls=%async_computation.1 | async-start | bytes 1048576 | tf_op jit(solution)/shard_map/psum | solution.py:53
  343.0 1.0 copy-start.3
  378.5 1.0 copy-start.2
  664.6 4.0 copy-start.5
Sparse Core Ops, SparseCore 0:
  173.3 129.0 all-reduce.2
  502.8 124.1 all-reduce.4
